TPU v7x, 512 devices: a whole 4x8x8 slice. The times are simulated.
512 devices in a mesh: seq: 64 (over z, x, y_lo), tensor: 8 (over y_hi, core).
Axes of the slice: x: 4, y: 8 (y_hi: 4, y_lo: 2; y = y_hi * 2 + y_lo), z: 8, core: 2. Of those that a mesh axis runs over, the one named last changes fastest.
Arguments:
- hidden_in: bfloat16 [8192, 2560], P('seq', 'tensor'), may hold values from -6 to 6
- norm_gain: float32 [2560], replicated, may hold values from 0.1 to 1.9
- w_query: bfloat16 [2560, 2048], P(None, 'tensor'), may hold values from -0.125 to 0.125
- w_key: bfloat16 [2560, 1024], P(None, 'tensor'), may hold values from -0.125 to 0.125
- w_value: bfloat16 [2560, 1024], P(None, 'tensor'), may hold values from -0.125 to 0.125
- w_out: bfloat16 [2048, 2560], P('tensor'), may hold values from -0.125 to 0.125
- q_gain: float32 [128], replicated, may hold values from 0.1 to 1.9
- k_gain: float32 [128], replicated, may hold values from 0.1 to 1.9
- lengths: int32 [16], replicated, may hold values from 1 to 6144, 8192 in all
Outputs:
- attn_out: bfloat16 [8192, 2560], P(('seq', 'tensor'))
- key_cache: bfloat16 [8192, 1024], P('seq', 'tensor')
- value_cache: bfloat16 [8192, 1024], P('seq', 'tensor')
Inputs may be any that keep to these rules, and one draw needn't show every extreme that they name: The lengths sum to 8192 and the largest is exactly 6144.
All inputs are finite; a program needn't handle non-finite values.
Results may differ from a plain program's by a relative error of at most 0.015.
Values may be sent and summed in bfloat16 or wider, within the bound.
No kernel may reach another device: no remote copies, remote signals or barrier semaphores. Data moves between devices by JAX's collectives and lax.ppermute only.
A program may use at most 64 MiB of HBM per device.

v0:
```python
import math
import jax
import jax.numpy as jnp
from jax import lax
from jax.sharding import Mesh
from jax.sharding import PartitionSpec as P

rope_base = 1000000.0
norm_eps = 1e-06
masked = -1e30
max_len = 6144
SEQ = ("z", "x", "ylo")
TEN = ("yhi", "core")


def prompt_starts(lengths, token_pos):
    ends = jnp.cumsum(lengths)
    starts = ends - lengths
    before = (ends[None, :] <= token_pos[:, None]).astype(jnp.int32)
    segment = jnp.sum(before, axis=1)
    onehot = segment[:, None] == jnp.arange(lengths.shape[0], dtype=jnp.int32)[None, :]
    return jnp.sum(jnp.where(onehot, starts[None, :], 0), axis=1)


def head_norm_rope(values, gain, rel_pos):
    width = values.shape[-1]
    half = width // 2
    mean_sq = jnp.mean(values * values, axis=-1, keepdims=True)
    normed = values * lax.rsqrt(mean_sq + norm_eps) * gain
    freq = rope_base ** (-jnp.arange(half, dtype=jnp.float32) * 2.0 / width)
    angle = rel_pos.astype(jnp.float32)[:, None] * freq[None, :]
    cosine = jnp.cos(angle)[:, None, :]
    sine = jnp.sin(angle)[:, None, :]
    first = normed[..., :half]
    second = normed[..., half:]
    return jnp.concatenate(
        [first * cosine - second * sine, second * cosine + first * sine], axis=-1
    )


def ring_pairs(n, k, forward, needed):
    out = []
    for src in range(n):
        if forward:
            start, dst = ((src - (k - 1)) % n, (src + 1) % n)
            reach = [(start + j) % n for j in range(k, n // 2 + 1)]
        else:
            start, dst = ((src + (k - 1)) % n, (src - 1) % n)
            reach = [(start - j) % n for j in range(k, n // 2 + 1)]
        if any((needed(start, d) for d in reach)):
            out.append((src, dst))
    return out


def ring_gather(piece, inner, name, stride, needed=lambda p, d: True):
    n = lax.axis_size(name)
    c = lax.axis_index(name)
    pieces, ids = ([piece], [c * stride + inner])
    a = b = piece
    if n % 2 == 0 and n >= 4:
        last = n // 2 - 1
        m = piece.shape[0]
        half = m // 2 if m % 2 == 0 else m
        for s in range(1, last + 1):
            if s == last:
                far = (c + n // 2) % n * stride
                ahead = [
                    (src, (src + 2) % n)
                    for src in range(n)
                    if needed((src - (last - 1)) % n, (src + 2) % n)
                ]
                pieces.append(lax.ppermute(a[:half], name, ahead))
                ids.append(far + inner[:half])
                if half < m:
                    behind = [
                        (src, (src - 2) % n)
                        for src in range(n)
                        if needed((src + (last - 1)) % n, (src - 2) % n)
                    ]
                    pieces.append(lax.ppermute(b[half:], name, behind))
                    ids.append(far + inner[half:])
            a = lax.ppermute(a, name, ring_pairs(n, s, True, needed))
            b = lax.ppermute(b, name, ring_pairs(n, s, False, needed))
            pieces += [a, b]
            ids += [(c - s) % n * stride + inner, (c + s) % n * stride + inner]
        return (jnp.concatenate(pieces, axis=0), jnp.concatenate(ids, axis=0))
    for s in range(1, (n - 1) // 2 + 1):
        a = lax.ppermute(a, name, ring_pairs(n, s, True, needed))
        b = lax.ppermute(b, name, ring_pairs(n, s, False, needed))
        pieces += [a, b]
        ids += [(c - s) % n * stride + inner, (c + s) % n * stride + inner]
    if n % 2 == 0:
        s = n // 2
        far = (c + s) % n * stride
        m = piece.shape[0]
        if m % 2 == 0:
            pieces += [
                lax.ppermute(a[: m // 2], name, ring_pairs(n, s, True, needed)),
                lax.ppermute(b[m // 2 :], name, ring_pairs(n, s, False, needed)),
            ]
            ids += [far + inner[: m // 2], far + inner[m // 2 :]]
        else:
            pieces += [lax.ppermute(a, name, ring_pairs(n, s, True, needed))]
            ids += [far + inner]
    return (jnp.concatenate(pieces, axis=0), jnp.concatenate(ids, axis=0))


def on_device(hidden_in, norm_gain, w_query, w_key, w_value, w_out, q_gain, k_gain, lengths):
    tokens = hidden_in.shape[0]
    width = w_query.shape[0]
    head_dim = q_gain.shape[0]
    q_cols = w_query.shape[1]
    kv_cols = w_key.shape[1]
    kv_local = kv_cols // head_dim
    group = q_cols // kv_cols
    combined = jnp.concatenate([w_query, w_key, w_value], axis=1)
    piece = lax.all_gather(hidden_in, TEN, axis=1, tiled=True)
    wide = piece.astype(jnp.float32)
    scaled = (wide * norm_gain[None, :]).astype(jnp.bfloat16)
    acc = jnp.dot(scaled, combined, preferred_element_type=jnp.float32)
    sumsq = jnp.sum(wide * wide, axis=1)
    proj = acc * lax.rsqrt(sumsq / width + norm_eps)[:, None]
    block_index = lax.axis_index(SEQ)
    token_pos = block_index * tokens + jnp.arange(tokens, dtype=jnp.int32)
    seg_start = prompt_starts(lengths, token_pos)
    rel_pos = token_pos - seg_start
    queries = head_norm_rope(
        proj[:, :q_cols].reshape(tokens, kv_local * group, head_dim), q_gain, rel_pos
    ).astype(jnp.bfloat16)
    keys = head_norm_rope(
        proj[:, q_cols : q_cols + kv_cols].reshape(tokens, kv_local, head_dim), k_gain, rel_pos
    ).astype(jnp.bfloat16)
    key_flat = keys.reshape(tokens, kv_cols)
    value_flat = proj[:, q_cols + kv_cols :].astype(jnp.bfloat16)
    nx, nlo = (lax.axis_size("x"), lax.axis_size("ylo"))
    piece = jnp.concatenate([key_flat, value_flat], axis=1)[None]
    block_ids = jnp.zeros((1,), jnp.int32)
    plane = nx * nlo
    piece = lax.all_to_all(
        jnp.broadcast_to(piece, (plane,) + piece.shape[1:]), ("x", "ylo"), 0, 0, tiled=True
    )
    block_ids = jnp.arange(plane, dtype=jnp.int32)
    back = -(--(-(max_len - 1) // tokens) // plane)
    piece, block_ids = ring_gather(piece, block_ids, "z", plane, lambda p, d: 1 <= d - p <= back)
    span = piece.shape[0] * tokens
    kv_all = piece.reshape(span, 2 * kv_cols)
    key_pos = (block_ids[:, None] * tokens + jnp.arange(tokens, dtype=jnp.int32)[None, :]).reshape(
        span
    )
    key_heads = kv_all[:, :kv_cols].reshape(span, kv_local, head_dim)
    value_heads = kv_all[:, kv_cols:].reshape(span, kv_local, head_dim)
    query_grid = queries.reshape(tokens, kv_local, group, head_dim)
    inv_root = 1.0 / math.sqrt(head_dim)
    score = (
        jnp.einsum("qhgd,khd->hgqk", query_grid, key_heads, preferred_element_type=jnp.float32)
        * inv_root
    )
    visible = (key_pos[None, :] >= seg_start[:, None]) & (key_pos[None, :] <= token_pos[:, None])
    score = jnp.where(visible[None, None], score, masked)
    top = jnp.max(score, axis=-1, keepdims=True)
    weights = jnp.where(visible[None, None], jnp.exp(score - top), 0.0)
    denom = jnp.sum(weights, axis=-1)
    summed = jnp.einsum(
        "hgqk,khd->hgqd",
        weights.astype(jnp.bfloat16),
        value_heads,
        preferred_element_type=jnp.float32,
    )
    attn = summed / denom[..., None]
    attn = jnp.transpose(attn, (2, 0, 1, 3)).reshape(tokens, q_cols).astype(jnp.bfloat16)
    part = jnp.dot(attn, w_out, preferred_element_type=jnp.float32).astype(jnp.bfloat16)
    nyhi = lax.axis_size("yhi")
    ncore = lax.axis_size("core")
    chunk = tokens // (nyhi * ncore)
    part = part.reshape(nyhi, ncore, chunk, -1).transpose(1, 0, 2, 3)
    part = lax.all_to_all(part, "core", 0, 0, tiled=True)
    part = jnp.sum(part.astype(jnp.float32), axis=0).astype(jnp.bfloat16)
    part = lax.all_to_all(part, "yhi", 0, 0, tiled=True)
    mixed = jnp.sum(part.astype(jnp.float32), axis=0).astype(jnp.bfloat16)
    return (mixed, key_flat, value_flat)


def solution(mesh):
    devices = mesh.devices
    nseq, nten = devices.shape
    nz = len({d.coords[2] for d in devices[:, 0]})
    nx = len({d.coords[0] for d in devices[:, 0]})
    ncore = len({d.core_on_chip for d in devices[0, :]})
    split = Mesh(devices.reshape(nz, nx, nseq // (nz * nx), nten // ncore, ncore), SEQ + TEN)
    seq, ten = (SEQ, TEN)
    placed = (
        P(seq, ten),
        P(),
        P(None, ten),
        P(None, ten),
        P(None, ten),
        P(ten, None),
        P(),
        P(),
        P(),
    )
    return jax.shard_map(
        on_device,
        mesh=split,
        in_specs=placed,
        out_specs=(P(seq + ten, None), P(seq, ten), P(seq, ten)),
        check_vma=False,
    )
```

profile of v0, /device:TPU:8, one launch (start us, length us, event | category | flops | bytes accessed | tf_op | source)
XLA Modules:
  0.0 132.9 jit_solution(4842833008063111337)
XLA Ops:
  0.7 17.5 %all_gather.3 = bf16[128,2560]{0,1:T(8,128)(2,1)S(1)} all-gather(bf16[128,320]{0,1:T(8,128)(2,1)} %param.9), channel_id=1, replica_groups=mesh['z'=8,'x'=4,'ylo'=2,'yhi'=4,'core'=2] {'yhi','core'}, dimensions={1}, use_global_device_ids=true | all-gather | bytes 737280 | tf_op jit(solution)/shard_map/all_gather | solution.py:117
  18.1 0.4 fusion.17
  18.5 3.1 %fusion.18 = f32[128,512]{1,0:T(8,128)S(1)} fusion(bf16[2560,128]{1,0:T(8,128)(2,1)} %param.13, bf16[2560,128]{1,0:T(8,128)(2,1)} %param.12, bf16[2560,256]{1,0:T(8,128)(2,1)} %param.11, bf16[128,2560]{0,1:T(8,128)(2,1)S(1)} %all_gather.3, f32[2560]{0:T(1024)} %param.10, f32[128]{0:T(128)S(1)} %add_rsqrt_fusion.2), kind=kOutput, calls=%fused_computation.25 | convolution fusion | flops 344457216 | bytes 3549696 | tf_op jit(solution)/shard_map/dot_general | solution.py:120
  22.8 0.8 broadcast_in_dim.31
  23.6 7.2 %all-to-all-start = ((bf16[8,128,256]{2,1,0:T(8,128)(2,1)}), bf16[8,128,256]{2,1,0:T(8,128)(2,1)S(1)}, u32[]{:S(2)}, u32[]{:S(2)}) async-start(bf16[8,128,256]{2,1,0:T(8,128)(2,1)} %broadcast_in_dim.31), calls=%async_computation | async-start | bytes 1048576 | tf_op jit(solution)/shard_map/all_to_all | solution.py:139
  31.2 0.7 reshape.365
  31.9 3.7 %compare_and_fusion = pred[128,8192]{0,1:T(8,128)(4,1)S(1)} fusion(s32[128]{0:T(128)S(1)} %iota_add_fusion, s32[128]{0:T(128)S(1)} %select_reduce_fusion, s32[8192]{0:T(1024)S(1)} %add_bitcast_fusion), kind=kLoop, calls=%fused_computation.11 | loop fusion | flops 3145728 | bytes 1082368 | tf_op jit(solution)/shard_map/and | solution.py:158
  35.7 4.9 %all-to-all-done = bf16[8,128,256]{2,1,0:T(8,128)(2,1)S(1)} async-done(((bf16[8,128,256]{2,1,0:T(8,128)(2,1)}), bf16[8,128,256]{2,1,0:T(8,128)(2,1)S(1)}, u32[]{:S(2)}, u32[]{:S(2)}) %all-to-all-start) | async-done | bytes 524320 | tf_op jit(solution)/shard_map/all_to_all | solution.py:139
  40.6 2.4 %collective-permute-start = (bf16[8,128,256]{2,1,0:T(8,128)(2,1)S(1)}, bf16[8,128,256]{2,1,0:T(8,128)(2,1)S(1)}, u32[]{:S(2)}, u32[]{:S(2)}) collective-permute-start(bf16[8,128,256]{2,1,0:T(8,128)(2,1)S(1)} %all-to-all-done), channel_id=1, source_target_pairs={{0,64},{64,128},{128,192},{192,256},{256,320},{320,384},{384,448},... | collective-permute-start | bytes 1572872 | tf_op jit(solution)/shard_map/ppermute | solution.py:82
  43.0 1.7 %multiply_reduce_fusion = f32[128,2]{1,0:T(8,128)} fusion(f32[128,2,128]{2,1,0:T(2,128)} %reshape.365), kind=kLoop, calls=%fused_computation.34 | loop fusion | flops 65280 | bytes 132096 | tf_op jit(solution)/shard_map/reduce_sum | solution.py:28
  44.7 0.9 copy.33
  45.6 8.3 %collective-permute-start.1 = (bf16[8,128,256]{2,1,0:T(8,128)(2,1)S(1)}, bf16[8,128,256]{2,1,0:T(8,128)(2,1)S(1)}, u32[]{:S(2)}, u32[]{:S(2)}) collective-permute-start(bf16[8,128,256]{2,1,0:T(8,128)(2,1)S(1)} %all-to-all-done), channel_id=1, source_target_pairs={{0,448},{64,0},{128,64},{192,128},{1,449},{65,1},{129,65},{193,129... | collective-permute-start | bytes 1572872 | tf_op jit(solution)/shard_map/ppermute | solution.py:83
  54.0 0.7 collective-permute-start.2
  55.0 9.2 %collective-permute-done.1 = bf16[8,128,256]{2,1,0:T(8,128)(2,1)S(1)} collective-permute-done((bf16[8,128,256]{2,1,0:T(8,128)(2,1)S(1)}, bf16[8,128,256]{2,1,0:T(8,128)(2,1)S(1)}, u32[]{:S(2)}, u32[]{:S(2)}) %collective-permute-start.1) | collective-permute-done | bytes 524320 | tf_op jit(solution)/shard_map/ppermute | solution.py:83
  64.2 5.6 %collective-permute-start.3 = (bf16[8,128,256]{2,1,0:T(8,128)(2,1)S(1)}, bf16[8,128,256]{2,1,0:T(8,128)(2,1)S(1)}, u32[]{:S(2)}, u32[]{:S(2)}) collective-permute-start(bf16[8,128,256]{2,1,0:T(8,128)(2,1)S(1)} %collective-permute-done.1), channel_id=1, source_target_pairs={{0,448},{64,0},{128,64},{448,384},{1,449},{65,1},{129,65},{449,385... | collective-permute-start | bytes 1572872 | tf_op jit(solution)/shard_map/ppermute | solution.py:83
  70.1 0.7 collective-permute-start.4
  70.7 0.7 collective-permute-start.6
  71.5 7.8 %collective-permute-done.3 = bf16[8,128,256]{2,1,0:T(8,128)(2,1)S(1)} collective-permute-done((bf16[8,128,256]{2,1,0:T(8,128)(2,1)S(1)}, bf16[8,128,256]{2,1,0:T(8,128)(2,1)S(1)}, u32[]{:S(2)}, u32[]{:S(2)}) %collective-permute-start.3) | collective-permute-done | bytes 524320 | tf_op jit(solution)/shard_map/ppermute | solution.py:83
  79.3 4.1 %collective-permute-start.5 = (bf16[4,128,256]{2,1,0:T(8,128)(2,1)S(1)}, bf16[4,128,256]{2,1,0:T(8,128)(2,1)S(1)}, u32[]{:S(2)}, u32[]{:S(2)}) collective-permute-start(bf16[4,128,256]{2,1,0:T(8,128)(2,1)S(1)} %slice.58), channel_id=1, source_target_pairs={{0,384},{64,448},{384,256},{448,320},{1,385},{65,449},{385,257},{4... | collective-permute-start | bytes 786440 | tf_op jit(solution)/shard_map/ppermute | solution.py:80
  83.5 3.9 %collective-permute-start.7 = (bf16[8,128,256]{2,1,0:T(8,128)(2,1)S(1)}, bf16[8,128,256]{2,1,0:T(8,128)(2,1)S(1)}, u32[]{:S(2)}, u32[]{:S(2)}) collective-permute-start(bf16[8,128,256]{2,1,0:T(8,128)(2,1)S(1)} %collective-permute-done.3), channel_id=1, source_target_pairs={{0,448},{64,0},{384,320},{448,384},{1,449},{65,1},{385,321},{449,3... | collective-permute-start | bytes 1572872 | tf_op jit(solution)/shard_map/ppermute | solution.py:83
  87.4 7.1 %collective-permute-done.5 = bf16[4,128,256]{2,1,0:T(8,128)(2,1)S(1)} collective-permute-done((bf16[4,128,256]{2,1,0:T(8,128)(2,1)S(1)}, bf16[4,128,256]{2,1,0:T(8,128)(2,1)S(1)}, u32[]{:S(2)}, u32[]{:S(2)}) %collective-permute-start.5) | collective-permute-done | bytes 262176 | tf_op jit(solution)/shard_map/ppermute | solution.py:80
  94.6 9.0 %collective-permute-done.7 = bf16[8,128,256]{2,1,0:T(8,128)(2,1)S(1)} collective-permute-done((bf16[8,128,256]{2,1,0:T(8,128)(2,1)S(1)}, bf16[8,128,256]{2,1,0:T(8,128)(2,1)S(1)}, u32[]{:S(2)}, u32[]{:S(2)}) %collective-permute-start.7) | collective-permute-done | bytes 524320 | tf_op jit(solution)/shard_map/ppermute | solution.py:83
  103.6 1.9 %fusion.47 = (f32[2,128]{1,0:T(2,128)S(1)}, f32[1,2,128,8192]{2,3,1,0:T(8,128)S(1)}) fusion(bf16[128,2,64]{2,0,1:T(8,128)(2,1)S(1)} %get-tuple-element.4, bf16[128,2,64]{2,0,1:T(8,128)(2,1)S(1)} %get-tuple-element.3, bf16[8192,256]{1,0:T(8,128)(2,1)S(1)} %bitcast.55, pred[128,8192]{0,1:T(8,128)(4,1)S(1)} %compare_and_fusion), kind=kOutput, calls=%fused_computation.91 | convolution fusion | flops 543293184 | bytes 11666432 | tf_op jit(solution)/shard_map/qhgd,khd->hgqk/dot_general | solution.py:155
  105.5 1.7 %fusion.2 = f32[2,128]{1,0:T(2,128)S(1)} fusion(f32[1,2,128,8192]{2,3,1,0:T(8,128)S(1)} %get-tuple-element.12, f32[2,128]{1,0:T(2,128)S(1)} %get-tuple-element.11, pred[128,8192]{0,1:T(8,128)(4,1)S(1)} %compare_and_fusion), kind=kLoop, calls=%fused_computation.4 | loop fusion | flops 6291200 | bytes 9439232 | tf_op jit(solution)/shard_map/reduce_sum | solution.py:162
  107.2 1.8 %fusion.24 = bf16[2,128,128]{1,2,0:T(8,128)(2,1)S(1)} fusion(bf16[8192,256]{1,0:T(8,128)(2,1)S(1)} %bitcast.56, f32[1,2,128,8192]{2,3,1,0:T(8,128)S(1)} %get-tuple-element.12, f32[2,128]{1,0:T(2,128)S(1)} %get-tuple-element.11, pred[128,8192]{0,1:T(8,128)(4,1)S(1)} %compare_and_fusion, f32[2,128]{1,0:T(2,128)S(1)} %fusion.2), kind=kOutput, calls=%fused_computation.27 | convolution fusion | flops 543227904 | bytes 11601920 | tf_op jit(solution)/shard_map/hgqk,khd->hgqd/dot_general | solution.py:163
  109.0 0.4 convolution_convert_fusion
  109.4 4.3 %all_to_all.15 = bf16[2,4,16,2560]{3,2,1,0:T(8,128)(2,1)S(1)} all-to-all(bf16[2,4,16,2560]{3,2,1,0:T(8,128)(2,1)S(1)} %bitcast.53), channel_id=1, replica_groups=mesh['z'=8,'x'=4,'ylo'=2,'yhi'=4,'core'=2] {'core'}, dimensions={0} | all-to-all | bytes 1310720 | tf_op jit(solution)/shard_map/all_to_all | solution.py:176
  113.7 0.9 reduce_sum.84
  114.6 4.6 %all-to-all-start.2 = ((bf16[4,16,2560]{2,1,0:T(8,128)(2,1)}), bf16[4,16,2560]{2,1,0:T(8,128)(2,1)S(1)}, u32[]{:S(2)}, u32[]{:S(2)}) async-start(bf16[4,16,2560]{2,1,0:T(8,128)(2,1)} %reduce_sum.84), calls=%async_computation.2 | async-start | bytes 655360 | tf_op jit(solution)/shard_map/all_to_all | solution.py:178
  119.2 0.7 pad_maximum_fusion.1
  119.9 12.3 %all-to-all-done.2 = bf16[4,16,2560]{2,1,0:T(8,128)(2,1)S(1)} async-done(((bf16[4,16,2560]{2,1,0:T(8,128)(2,1)}), bf16[4,16,2560]{2,1,0:T(8,128)(2,1)S(1)}, u32[]{:S(2)}, u32[]{:S(2)}) %all-to-all-start.2) | async-done | bytes 327712 | tf_op jit(solution)/shard_map/all_to_all | solution.py:178
  132.2 0.7 reduce_sum.85
  (65 shorter events, 2.3 us)
Async XLA Ops:
  0.6 108.4 %copy-start = (bf16[256,2560]{1,0:T(8,128)(2,1)S(1)}, bf16[256,2560]{1,0:T(8,128)(2,1)}, u32[]{:S(2)}) copy-start(bf16[256,2560]{1,0:T(8,128)(2,1)} %param.14) | copy-start | bytes 3932164
  18.1 3.6 %copy-start.8 = (s32[16]{0:T(128)S(1)}, s32[16]{0:T(128)}, u32[]{:S(2)}) copy-start(s32[16]{0:T(128)} %param.17) | copy-start | bytes 196
  18.1 4.1 %copy-start.6 = (f32[128]{0:T(128)S(1)}, f32[128]{0:T(128)}, u32[]{:S(2)}) copy-start(f32[128]{0:T(128)} %param.16) | copy-start | bytes 1540
  21.6 32.3 %copy-start.7 = (f32[128]{0:T(128)S(1)}, f32[128]{0:T(128)}, u32[]{:S(2)}) copy-start(f32[128]{0:T(128)} %param.15) | copy-start | bytes 1540
  21.7 9.1 %copy-start.5 = (bf16[128,128]{1,0:T(8,128)(2,1)}, bf16[128,128]{1,0:T(8,128)(2,1)S(1)}, u32[]{:S(2)}) copy-start(bf16[128,128]{1,0:T(8,128)(2,1)S(1)} %slice.94) | copy-start | bytes 98308
  22.6 0.9 copy-start.1
  22.6 0.9 copy-start.3
  23.6 17.0 %all-to-all-start = ((bf16[8,128,256]{2,1,0:T(8,128)(2,1)}), bf16[8,128,256]{2,1,0:T(8,128)(2,1)S(1)}, u32[]{:S(2)}, u32[]{:S(2)}) async-start(bf16[8,128,256]{2,1,0:T(8,128)(2,1)} %broadcast_in_dim.31), calls=%async_computation | async-start | bytes 1048576 | tf_op jit(solution)/shard_map/all_to_all | solution.py:139
  40.6 13.5 %collective-permute-start = (bf16[8,128,256]{2,1,0:T(8,128)(2,1)S(1)}, bf16[8,128,256]{2,1,0:T(8,128)(2,1)S(1)}, u32[]{:S(2)}, u32[]{:S(2)}) collective-permute-start(bf16[8,128,256]{2,1,0:T(8,128)(2,1)S(1)} %all-to-all-done), channel_id=1, source_target_pairs={{0,64},{64,128},{128,192},{192,256},{256,320},{320,384},{384,448},... | collective-permute-start | bytes 1572872 | tf_op jit(solution)/shard_map/ppermute | solution.py:82
  45.6 18.6 %collective-permute-start.1 = (bf16[8,128,256]{2,1,0:T(8,128)(2,1)S(1)}, bf16[8,128,256]{2,1,0:T(8,128)(2,1)S(1)}, u32[]{:S(2)}, u32[]{:S(2)}) collective-permute-start(bf16[8,128,256]{2,1,0:T(8,128)(2,1)S(1)} %all-to-all-done), channel_id=1, source_target_pairs={{0,448},{64,0},{128,64},{192,128},{1,449},{65,1},{129,65},{193,129... | collective-permute-start | bytes 1572872 | tf_op jit(solution)/shard_map/ppermute | solution.py:83
  54.0 16.0 %collective-permute-start.2 = (bf16[8,128,256]{2,1,0:T(8,128)(2,1)S(1)}, bf16[8,128,256]{2,1,0:T(8,128)(2,1)S(1)}, u32[]{:S(2)}, u32[]{:S(2)}) collective-permute-start(bf16[8,128,256]{2,1,0:T(8,128)(2,1)S(1)} %collective-permute-done), channel_id=1, source_target_pairs={{64,128},{128,192},{192,256},{256,320},{320,384},{384,448},{65,129... | collective-permute-start | bytes 1572872 | tf_op jit(solution)/shard_map/ppermute | solution.py:82
  64.2 15.1 %collective-permute-start.3 = (bf16[8,128,256]{2,1,0:T(8,128)(2,1)S(1)}, bf16[8,128,256]{2,1,0:T(8,128)(2,1)S(1)}, u32[]{:S(2)}, u32[]{:S(2)}) collective-permute-start(bf16[8,128,256]{2,1,0:T(8,128)(2,1)S(1)} %collective-permute-done.1), channel_id=1, source_target_pairs={{0,448},{64,0},{128,64},{448,384},{1,449},{65,1},{129,65},{449,385... | collective-permute-start | bytes 1572872 | tf_op jit(solution)/shard_map/ppermute | solution.py:83
  70.1 17.3 %collective-permute-start.4 = (bf16[4,128,256]{2,1,0:T(8,128)(2,1)S(1)}, bf16[4,128,256]{2,1,0:T(8,128)(2,1)S(1)}, u32[]{:S(2)}, u32[]{:S(2)}) collective-permute-start(bf16[4,128,256]{2,1,0:T(8,128)(2,1)S(1)} %slice.57), channel_id=1, source_target_pairs={{128,256},{192,320},{256,384},{320,448},{129,257},{193,321},{257,3... | collective-permute-start | bytes 786440 | tf_op jit(solution)/shard_map/ppermute | solution.py:72
  70.7 23.8 %collective-permute-start.6 = (bf16[8,128,256]{2,1,0:T(8,128)(2,1)S(1)}, bf16[8,128,256]{2,1,0:T(8,128)(2,1)S(1)}, u32[]{:S(2)}, u32[]{:S(2)}) collective-permute-start(bf16[8,128,256]{2,1,0:T(8,128)(2,1)S(1)} %collective-permute-done.2), channel_id=1, source_target_pairs={{128,192},{192,256},{256,320},{320,384},{384,448},{129,193},{193,2... | collective-permute-start | bytes 1572872 | tf_op jit(solution)/shard_map/ppermute | solution.py:82
  79.3 15.2 %collective-permute-start.5 = (bf16[4,128,256]{2,1,0:T(8,128)(2,1)S(1)}, bf16[4,128,256]{2,1,0:T(8,128)(2,1)S(1)}, u32[]{:S(2)}, u32[]{:S(2)}) collective-permute-start(bf16[4,128,256]{2,1,0:T(8,128)(2,1)S(1)} %slice.58), channel_id=1, source_target_pairs={{0,384},{64,448},{384,256},{448,320},{1,385},{65,449},{385,257},{4... | collective-permute-start | bytes 786440 | tf_op jit(solution)/shard_map/ppermute | solution.py:80
  83.5 20.1 %collective-permute-start.7 = (bf16[8,128,256]{2,1,0:T(8,128)(2,1)S(1)}, bf16[8,128,256]{2,1,0:T(8,128)(2,1)S(1)}, u32[]{:S(2)}, u32[]{:S(2)}) collective-permute-start(bf16[8,128,256]{2,1,0:T(8,128)(2,1)S(1)} %collective-permute-done.3), channel_id=1, source_target_pairs={{0,448},{64,0},{384,320},{448,384},{1,449},{65,1},{385,321},{449,3... | collective-permute-start | bytes 1572872 | tf_op jit(solution)/shard_map/ppermute | solution.py:83
  109.0 10.2 %copy-start.2 = (bf16[128,64]{1,0:T(8,128)(2,1)S(1)}, bf16[128,64]{1,0:T(8,128)(2,1)}, u32[]{:S(2)}) copy-start(bf16[128,64]{1,0:T(8,128)(2,1)} %copy-done.1) | copy-start | bytes 49156
  109.0 10.2 %copy-start.4 = (bf16[128,64]{1,0:T(8,128)(2,1)S(1)}, bf16[128,64]{1,0:T(8,128)(2,1)}, u32[]{:S(2)}) copy-start(bf16[128,64]{1,0:T(8,128)(2,1)} %copy-done.3) | copy-start | bytes 49156
  114.6 17.7 %all-to-all-start.2 = ((bf16[4,16,2560]{2,1,0:T(8,128)(2,1)}), bf16[4,16,2560]{2,1,0:T(8,128)(2,1)S(1)}, u32[]{:S(2)}, u32[]{:S(2)}) async-start(bf16[4,16,2560]{2,1,0:T(8,128)(2,1)} %reduce_sum.84), calls=%async_computation.2 | async-start | bytes 655360 | tf_op jit(solution)/shard_map/all_to_all | solution.py:178
where the time goes:
time: 134 us; the launch traced here: 133 us
  waiting for transfers between devices  50.3 us (38%)
  starting transfers between devices  38.2 us (29%)
  blocking collectives  21.7 us (16%)
  other arithmetic  11.4 us (9%)
  matrix products  7.1 us (5%)
  local copies, waits for them, and re-layouts  3.07 us (2%)
    ppermute x3, waiting for transfers between devices, ring_gather(): b = lax.ppermute(b, name, ring_pairs(n, s, False, needed))  26 us
    ppermute x3, starting transfers between devices, ring_gather(): b = lax.ppermute(b, name, ring_pairs(n, s, False, needed))  17.7 us
    all_gather x1, blocking collectives, on_device(): piece = lax.all_gather(hidden_in, TEN, axis=1, tiled=True)  17.5 us
    all_to_all x1, waiting for transfers between devices, on_device(): part = lax.all_to_all(part, 'yhi', 0, 0, tiled=True)  12.3 us
    all_to_all x1, starting transfers between devices, on_device(): lax.all_to_all(jnp.broadcast_to(piece, (plane,) + piece.shape[1:]), ('x',...  7.23 us
    ppermute x1, waiting for transfers between devices, ring_gather(): pieces.append(lax.ppermute(b[half:], name, behind))  7.1 us
    all_to_all x1, waiting for transfers between devices, on_device(): lax.all_to_all(jnp.broadcast_to(piece, (plane,) + piece.shape[1:]), ('x',...  4.9 us
    all_to_all x1, starting transfers between devices, on_device(): part = lax.all_to_all(part, 'yhi', 0, 0, tiled=True)  4.64 us
  transfers between devices with their start and end apart: 10, of which 6 were waited for; matrix products, arithmetic and copies ran while one was open for 7% of the time, Pallas kernels for 0%

commit v1 on v0

--- a/solution.py
+++ b/solution.py
@@ -114,7 +114,14 @@
     kv_local = kv_cols // head_dim
     group = q_cols // kv_cols
     combined = jnp.concatenate([w_query, w_key, w_value], axis=1)
-    piece = lax.all_gather(hidden_in, TEN, axis=1, tiled=True)
+
+    def close_blocks_in(local):
+        a_now = jnp.concatenate(
+            lax.all_to_all(jnp.stack(lax.axis_size(TEN) * [local]), TEN, 0, 0), axis=1
+        )
+        return a_now
+
+    piece = close_blocks_in(hidden_in)
     wide = piece.astype(jnp.float32)
     scaled = (wide * norm_gain[None, :]).astype(jnp.bfloat16)
     acc = jnp.dot(scaled, combined, preferred_element_type=jnp.float32)

time: 134 us -> 138 us (1.030)
  the two profiles are of different devices: /device:TPU:8 before, /device:TPU:17 now
where the time goes in v1:
time: 138 us; the launch traced here: 137 us
  waiting for transfers between devices  55.1 us (40%)
  starting transfers between devices  47.3 us (34%)
  other arithmetic  14.7 us (11%)
  local copies, waits for them, and re-layouts  6.7 us (5%)
  blocking collectives  6.29 us (5%)
  matrix products  6.1 us (4%)
    ppermute x3, waiting for transfers between devices, ring_gather(): b = lax.ppermute(b, name, ring_pairs(n, s, False, needed))  23 us
    ppermute x3, starting transfers between devices, ring_gather(): b = lax.ppermute(b, name, ring_pairs(n, s, False, needed))  16.2 us
    all_to_all x1, waiting for transfers between devices, close_blocks_in(): lax.all_to_all(jnp.stack(lax.axis_size(TEN) * [local]), TEN, 0, 0)  13.9 us
    all_to_all x1, waiting for transfers between devices, on_device(): part = lax.all_to_all(part, 'yhi', 0, 0, tiled=True)  10.4 us
    all_to_all x1, starting transfers between devices, close_blocks_in(): lax.all_to_all(jnp.stack(lax.axis_size(TEN) * [local]), TEN, 0, 0)  9.42 us
    all_to_all x1, blocking collectives, on_device(): part = lax.all_to_all(part, 'core', 0, 0, tiled=True)  6.29 us
    ppermute x3, starting transfers between devices, ring_gather(): a = lax.ppermute(a, name, ring_pairs(n, s, True, needed))  6.17 us
    ppermute x1, starting transfers between devices, ring_gather(): pieces.append(lax.ppermute(b[half:], name, behind))  5.67 us
  transfers between devices with their start and end apart: 11, of which 7 were waited for; matrix products, arithmetic and copies ran while one was open for 10% of the time, Pallas kernels for 0%

profile of v1, /device:TPU:17, one launch (start us, length us, event | category | flops | bytes accessed | tf_op | source)
XLA Modules:
  0.0 137.2 jit_solution(1110182268932040493)
XLA Ops:
  0.7 1.9 %stack.2 = bf16[8,128,320]{1,2,0:T(8,128)(2,1)} broadcast(bf16[128,320]{0,1:T(8,128)(2,1)} %param.9), dimensions={1,2} | broadcast | bytes 737280 | tf_op jit(solution)/shard_map/stack | solution.py:120
  2.6 9.4 %all-to-all-start = ((bf16[8,128,320]{1,2,0:T(8,128)(2,1)}), bf16[8,128,320]{1,2,0:T(8,128)(2,1)S(1)}, u32[]{:S(2)}, u32[]{:S(2)}) async-start(bf16[8,128,320]{1,2,0:T(8,128)(2,1)} %stack.2), calls=%async_computation | async-start | bytes 1310720 | tf_op jit(solution)/shard_map/all_to_all | solution.py:120
  12.1 0.7 copy.33
  14.1 13.9 %all-to-all-done = bf16[8,128,320]{1,2,0:T(8,128)(2,1)S(1)} async-done(((bf16[8,128,320]{1,2,0:T(8,128)(2,1)}), bf16[8,128,320]{1,2,0:T(8,128)(2,1)S(1)}, u32[]{:S(2)}, u32[]{:S(2)}) %all-to-all-start) | async-done | bytes 655392 | tf_op jit(solution)/shard_map/all_to_all | solution.py:120
  28.3 1.1 fusion.16
  29.4 2.1 %fusion.17 = f32[128,512]{1,0:T(8,128)S(1)} fusion(bf16[128,2560]{0,1:T(8,128)(2,1)S(1)} %fusion.16, bf16[2560,128]{1,0:T(8,128)(2,1)S(1)} %copy-done.8, bf16[2560,128]{1,0:T(8,128)(2,1)} %param.12, bf16[2560,256]{1,0:T(8,128)(2,1)} %param.11, f32[128]{0:T(128)S(1)} %add_rsqrt_fusion.2), kind=kOutput, calls=%fused_computation.24 | convolution fusion | flops 343474176 | bytes 3539456 | tf_op jit(solution)/shard_map/dot_general | solution.py:127
  32.2 0.8 broadcast_in_dim.31
  33.1 4.4 %all-to-all-start.1 = ((bf16[8,128,256]{2,1,0:T(8,128)(2,1)}), bf16[8,128,256]{2,1,0:T(8,128)(2,1)S(1)}, u32[]{:S(2)}, u32[]{:S(2)}) async-start(bf16[8,128,256]{2,1,0:T(8,128)(2,1)} %broadcast_in_dim.31), calls=%async_computation.1 | async-start | bytes 1048576 | tf_op jit(solution)/shard_map/all_to_all | solution.py:146
  37.4 3.7 %compare_and_fusion = pred[128,8192]{0,1:T(8,128)(4,1)S(1)} fusion(s32[128]{0:T(128)S(1)} %iota_add_fusion, s32[128]{0:T(128)S(1)} %select_reduce_fusion, s32[8192]{0:T(1024)S(1)} %add_bitcast_fusion), kind=kLoop, calls=%fused_computation.11 | loop fusion | flops 3145728 | bytes 1082368 | tf_op jit(solution)/shard_map/and | solution.py:165
  41.1 0.9 multiply_cosine_fusion
  42.1 4.0 %all-to-all-done.1 = bf16[8,128,256]{2,1,0:T(8,128)(2,1)S(1)} async-done(((bf16[8,128,256]{2,1,0:T(8,128)(2,1)}), bf16[8,128,256]{2,1,0:T(8,128)(2,1)S(1)}, u32[]{:S(2)}, u32[]{:S(2)}) %all-to-all-start.1) | async-done | bytes 524320 | tf_op jit(solution)/shard_map/all_to_all | solution.py:146
  46.1 4.8 %collective-permute-start = (bf16[8,128,256]{2,1,0:T(8,128)(2,1)S(1)}, bf16[8,128,256]{2,1,0:T(8,128)(2,1)}, u32[]{:S(2)}, u32[]{:S(2)}) collective-permute-start(bf16[8,128,256]{2,1,0:T(8,128)(2,1)S(1)} %all-to-all-done.1), channel_id=1, source_target_pairs={{0,64},{64,128},{128,192},{192,256},{256,320},{320,384},{384,448},... | collective-permute-start | bytes 1572872 | tf_op jit(solution)/shard_map/ppermute | solution.py:82
  50.9 0.7 reshape.371
  51.6 7.2 %collective-permute-start.1 = (bf16[8,128,256]{2,1,0:T(8,128)(2,1)S(1)}, bf16[8,128,256]{2,1,0:T(8,128)(2,1)S(1)}, u32[]{:S(2)}, u32[]{:S(2)}) collective-permute-start(bf16[8,128,256]{2,1,0:T(8,128)(2,1)S(1)} %all-to-all-done.1), channel_id=1, source_target_pairs={{0,448},{64,0},{128,64},{192,128},{1,449},{65,1},{129,65},{193,129... | collective-permute-start | bytes 1572872 | tf_op jit(solution)/shard_map/ppermute | solution.py:83
  58.8 1.7 %multiply_reduce_fusion.1 = f32[128,2]{1,0:T(8,128)} fusion(f32[128,2,128]{2,1,0:T(2,128)} %reshape.371), kind=kLoop, calls=%fused_computation.32 | loop fusion | flops 65280 | bytes 132096 | tf_op jit(solution)/shard_map/reduce_sum | solution.py:28
  60.5 0.9 copy.34
  62.3 5.4 %collective-permute-done.1 = bf16[8,128,256]{2,1,0:T(8,128)(2,1)S(1)} collective-permute-done((bf16[8,128,256]{2,1,0:T(8,128)(2,1)S(1)}, bf16[8,128,256]{2,1,0:T(8,128)(2,1)S(1)}, u32[]{:S(2)}, u32[]{:S(2)}) %collective-permute-start.1) | collective-permute-done | bytes 524320 | tf_op jit(solution)/shard_map/ppermute | solution.py:83
  67.7 5.3 %collective-permute-start.3 = (bf16[8,128,256]{2,1,0:T(8,128)(2,1)S(1)}, bf16[8,128,256]{2,1,0:T(8,128)(2,1)S(1)}, u32[]{:S(2)}, u32[]{:S(2)}) collective-permute-start(bf16[8,128,256]{2,1,0:T(8,128)(2,1)S(1)} %collective-permute-done.1), channel_id=1, source_target_pairs={{0,448},{64,0},{128,64},{448,384},{1,449},{65,1},{129,65},{449,385... | collective-permute-start | bytes 1572872 | tf_op jit(solution)/shard_map/ppermute | solution.py:83
  73.0 1.0 subtract_convert_fusion
  74.0 1.1 constant_dynamic-update-slice_fusion.7
  76.6 4.5 %collective-permute-done.3 = bf16[8,128,256]{2,1,0:T(8,128)(2,1)S(1)} collective-permute-done((bf16[8,128,256]{2,1,0:T(8,128)(2,1)S(1)}, bf16[8,128,256]{2,1,0:T(8,128)(2,1)S(1)}, u32[]{:S(2)}, u32[]{:S(2)}) %collective-permute-start.3) | collective-permute-done | bytes 524320 | tf_op jit(solution)/shard_map/ppermute | solution.py:83
  81.1 5.7 %collective-permute-start.5 = (bf16[4,128,256]{2,1,0:T(8,128)(2,1)S(1)}, bf16[4,128,256]{2,1,0:T(8,128)(2,1)S(1)}, u32[]{:S(2)}, u32[]{:S(2)}) collective-permute-start(bf16[4,128,256]{2,1,0:T(8,128)(2,1)S(1)} %slice.58), channel_id=1, source_target_pairs={{0,384},{64,448},{384,256},{448,320},{1,385},{65,449},{385,257},{4... | collective-permute-start | bytes 786440 | tf_op jit(solution)/shard_map/ppermute | solution.py:80
  86.7 3.7 %collective-permute-start.7 = (bf16[8,128,256]{2,1,0:T(8,128)(2,1)S(1)}, bf16[8,128,256]{2,1,0:T(8,128)(2,1)S(1)}, u32[]{:S(2)}, u32[]{:S(2)}) collective-permute-start(bf16[8,128,256]{2,1,0:T(8,128)(2,1)S(1)} %collective-permute-done.3), channel_id=1, source_target_pairs={{0,448},{64,0},{384,320},{448,384},{1,449},{65,1},{385,321},{449,3... | collective-permute-start | bytes 1572872 | tf_op jit(solution)/shard_map/ppermute | solution.py:83
  90.6 3.9 %collective-permute-done.5 = bf16[4,128,256]{2,1,0:T(8,128)(2,1)S(1)} collective-permute-done((bf16[4,128,256]{2,1,0:T(8,128)(2,1)S(1)}, bf16[4,128,256]{2,1,0:T(8,128)(2,1)S(1)}, u32[]{:S(2)}, u32[]{:S(2)}) %collective-permute-start.5) | collective-permute-done | bytes 262176 | tf_op jit(solution)/shard_map/ppermute | solution.py:80
  94.5 13.2 %collective-permute-done.7 = bf16[8,128,256]{2,1,0:T(8,128)(2,1)S(1)} collective-permute-done((bf16[8,128,256]{2,1,0:T(8,128)(2,1)S(1)}, bf16[8,128,256]{2,1,0:T(8,128)(2,1)S(1)}, u32[]{:S(2)}, u32[]{:S(2)}) %collective-permute-start.7) | collective-permute-done | bytes 524320 | tf_op jit(solution)/shard_map/ppermute | solution.py:83
  107.7 1.9 %fusion.44 = (f32[2,128]{1,0:T(2,128)S(1)}, f32[1,2,128,8192]{2,3,1,0:T(8,128)S(1)}) fusion(bf16[128,2,64]{2,0,1:T(8,128)(2,1)S(1)} %get-tuple-element.4, bf16[128,2,64]{2,0,1:T(8,128)(2,1)S(1)} %get-tuple-element.3, bf16[8192,256]{1,0:T(8,128)(2,1)S(1)} %bitcast.62, pred[128,8192]{0,1:T(8,128)(4,1)S(1)} %compare_and_fusion), kind=kOutput, calls=%fused_computation.89 | convolution fusion | flops 543293184 | bytes 11666432 | tf_op jit(solution)/shard_map/qhgd,khd->hgqk/dot_general | solution.py:162
  109.6 1.7 %fusion.2 = f32[2,128]{1,0:T(2,128)S(1)} fusion(f32[1,2,128,8192]{2,3,1,0:T(8,128)S(1)} %get-tuple-element.12, f32[2,128]{1,0:T(2,128)S(1)} %get-tuple-element.11, pred[128,8192]{0,1:T(8,128)(4,1)S(1)} %compare_and_fusion), kind=kLoop, calls=%fused_computation.4 | loop fusion | flops 6291200 | bytes 9439232 | tf_op jit(solution)/shard_map/reduce_sum | solution.py:169
  111.3 1.8 %fusion.23 = bf16[2,128,128]{1,2,0:T(8,128)(2,1)S(1)} fusion(bf16[8192,256]{1,0:T(8,128)(2,1)S(1)} %bitcast.63, f32[1,2,128,8192]{2,3,1,0:T(8,128)S(1)} %get-tuple-element.12, f32[2,128]{1,0:T(2,128)S(1)} %get-tuple-element.11, pred[128,8192]{0,1:T(8,128)(4,1)S(1)} %compare_and_fusion, f32[2,128]{1,0:T(2,128)S(1)} %fusion.2), kind=kOutput, calls=%fused_computation.26 | convolution fusion | flops 543227904 | bytes 11601920 | tf_op jit(solution)/shard_map/hgqk,khd->hgqd/dot_general | solution.py:170
  113.5 6.3 %all_to_all.20 = bf16[2,4,16,2560]{3,2,1,0:T(8,128)(2,1)S(1)} all-to-all(bf16[2,4,16,2560]{3,2,1,0:T(8,128)(2,1)S(1)} %bitcast.60), channel_id=1, replica_groups=mesh['z'=8,'x'=4,'ylo'=2,'yhi'=4,'core'=2] {'core'}, dimensions={0} | all-to-all | bytes 1310720 | tf_op jit(solution)/shard_map/all_to_all | solution.py:183
  119.8 0.9 reduce_sum.84
  120.7 4.8 %all-to-all-start.3 = ((bf16[4,16,2560]{2,1,0:T(8,128)(2,1)}), bf16[4,16,2560]{2,1,0:T(8,128)(2,1)S(1)}, u32[]{:S(2)}, u32[]{:S(2)}) async-start(bf16[4,16,2560]{2,1,0:T(8,128)(2,1)} %reduce_sum.84), calls=%async_computation.3 | async-start | bytes 655360 | tf_op jit(solution)/shard_map/all_to_all | solution.py:185
  126.2 10.4 %all-to-all-done.3 = bf16[4,16,2560]{2,1,0:T(8,128)(2,1)S(1)} async-done(((bf16[4,16,2560]{2,1,0:T(8,128)(2,1)}), bf16[4,16,2560]{2,1,0:T(8,128)(2,1)S(1)}, u32[]{:S(2)}, u32[]{:S(2)}) %all-to-all-start.3) | async-done | bytes 327712 | tf_op jit(solution)/shard_map/all_to_all | solution.py:185
  (68 shorter events, 6.6 us)
Async XLA Ops:
  0.6 112.5 %copy-start = (bf16[256,2560]{1,0:T(8,128)(2,1)S(1)}, bf16[256,2560]{1,0:T(8,128)(2,1)}, u32[]{:S(2)}) copy-start(bf16[256,2560]{1,0:T(8,128)(2,1)} %param.14) | copy-start | bytes 3932164
  0.6 28.8 %copy-start.8 = (bf16[2560,128]{1,0:T(8,128)(2,1)S(1)}, bf16[2560,128]{1,0:T(8,128)(2,1)}, u32[]{:S(2)}) copy-start(bf16[2560,128]{1,0:T(8,128)(2,1)} %param.13) | copy-start | bytes 1966084
  2.6 25.3 %all-to-all-start = ((bf16[8,128,320]{1,2,0:T(8,128)(2,1)}), bf16[8,128,320]{1,2,0:T(8,128)(2,1)S(1)}, u32[]{:S(2)}, u32[]{:S(2)}) async-start(bf16[8,128,320]{1,2,0:T(8,128)(2,1)} %stack.2), calls=%async_computation | async-start | bytes 1310720 | tf_op jit(solution)/shard_map/all_to_all | solution.py:120
  28.3 3.4 %copy-start.6 = (f32[128]{0:T(128)S(1)}, f32[128]{0:T(128)}, u32[]{:S(2)}) copy-start(f32[128]{0:T(128)} %param.16) | copy-start | bytes 1540
  29.4 32.7 %copy-start.7 = (f32[128]{0:T(128)S(1)}, f32[128]{0:T(128)}, u32[]{:S(2)}) copy-start(f32[128]{0:T(128)} %param.15) | copy-start | bytes 1540
  31.7 1.4 %copy-start.5 = (bf16[128,128]{1,0:T(8,128)(2,1)}, bf16[128,128]{1,0:T(8,128)(2,1)S(1)}, u32[]{:S(2)}) copy-start(bf16[128,128]{1,0:T(8,128)(2,1)S(1)} %slice.94) | copy-start | bytes 98308
  32.1 0.9 copy-start.1
  32.1 0.9 copy-start.3
  33.1 13.0 %all-to-all-start.1 = ((bf16[8,128,256]{2,1,0:T(8,128)(2,1)}), bf16[8,128,256]{2,1,0:T(8,128)(2,1)S(1)}, u32[]{:S(2)}, u32[]{:S(2)}) async-start(bf16[8,128,256]{2,1,0:T(8,128)(2,1)} %broadcast_in_dim.31), calls=%async_computation.1 | async-start | bytes 1048576 | tf_op jit(solution)/shard_map/all_to_all | solution.py:146
  46.1 15.4 %collective-permute-start = (bf16[8,128,256]{2,1,0:T(8,128)(2,1)S(1)}, bf16[8,128,256]{2,1,0:T(8,128)(2,1)}, u32[]{:S(2)}, u32[]{:S(2)}) collective-permute-start(bf16[8,128,256]{2,1,0:T(8,128)(2,1)S(1)} %all-to-all-done.1), channel_id=1, source_target_pairs={{0,64},{64,128},{128,192},{192,256},{256,320},{320,384},{384,448},... | collective-permute-start | bytes 1572872 | tf_op jit(solution)/shard_map/ppermute | solution.py:82
  51.6 16.1 %collective-permute-start.1 = (bf16[8,128,256]{2,1,0:T(8,128)(2,1)S(1)}, bf16[8,128,256]{2,1,0:T(8,128)(2,1)S(1)}, u32[]{:S(2)}, u32[]{:S(2)}) collective-permute-start(bf16[8,128,256]{2,1,0:T(8,128)(2,1)S(1)} %all-to-all-done.1), channel_id=1, source_target_pairs={{0,448},{64,0},{128,64},{192,128},{1,449},{65,1},{129,65},{193,129... | collective-permute-start | bytes 1572872 | tf_op jit(solution)/shard_map/ppermute | solution.py:83
  61.5 13.6 %collective-permute-start.2 = (bf16[8,128,256]{2,1,0:T(8,128)(2,1)}, bf16[8,128,256]{2,1,0:T(8,128)(2,1)S(1)}, u32[]{:S(2)}, u32[]{:S(2)}) collective-permute-start(bf16[8,128,256]{2,1,0:T(8,128)(2,1)} %collective-permute-done), channel_id=1, source_target_pairs={{64,128},{128,192},{192,256},{256,320},{320,384},{384,448},{65,129... | collective-permute-start | bytes 1572872 | tf_op jit(solution)/shard_map/ppermute | solution.py:82
  67.7 13.3 %collective-permute-start.3 = (bf16[8,128,256]{2,1,0:T(8,128)(2,1)S(1)}, bf16[8,128,256]{2,1,0:T(8,128)(2,1)S(1)}, u32[]{:S(2)}, u32[]{:S(2)}) collective-permute-start(bf16[8,128,256]{2,1,0:T(8,128)(2,1)S(1)} %collective-permute-done.1), channel_id=1, source_target_pairs={{0,448},{64,0},{128,64},{448,384},{1,449},{65,1},{129,65},{449,385... | collective-permute-start | bytes 1572872 | tf_op jit(solution)/shard_map/ppermute | solution.py:83
  75.1 15.4 %collective-permute-start.4 = (bf16[4,128,256]{2,1,0:T(8,128)(2,1)S(1)}, bf16[4,128,256]{2,1,0:T(8,128)(2,1)S(1)}, u32[]{:S(2)}, u32[]{:S(2)}) collective-permute-start(bf16[4,128,256]{2,1,0:T(8,128)(2,1)S(1)} %slice.57), channel_id=1, source_target_pairs={{128,256},{192,320},{256,384},{320,448},{129,257},{193,321},{257,3... | collective-permute-start | bytes 786440 | tf_op jit(solution)/shard_map/ppermute | solution.py:72
  75.8 18.6 %collective-permute-start.6 = (bf16[8,128,256]{2,1,0:T(8,128)(2,1)S(1)}, bf16[8,128,256]{2,1,0:T(8,128)(2,1)S(1)}, u32[]{:S(2)}, u32[]{:S(2)}) collective-permute-start(bf16[8,128,256]{2,1,0:T(8,128)(2,1)S(1)} %collective-permute-done.2), channel_id=1, source_target_pairs={{128,192},{192,256},{256,320},{320,384},{384,448},{129,193},{193,2... | collective-permute-start | bytes 1572872 | tf_op jit(solution)/shard_map/ppermute | solution.py:82
  81.1 13.4 %collective-permute-start.5 = (bf16[4,128,256]{2,1,0:T(8,128)(2,1)S(1)}, bf16[4,128,256]{2,1,0:T(8,128)(2,1)S(1)}, u32[]{:S(2)}, u32[]{:S(2)}) collective-permute-start(bf16[4,128,256]{2,1,0:T(8,128)(2,1)S(1)} %slice.58), channel_id=1, source_target_pairs={{0,384},{64,448},{384,256},{448,320},{1,385},{65,449},{385,257},{4... | collective-permute-start | bytes 786440 | tf_op jit(solution)/shard_map/ppermute | solution.py:80
  86.7 20.9 %collective-permute-start.7 = (bf16[8,128,256]{2,1,0:T(8,128)(2,1)S(1)}, bf16[8,128,256]{2,1,0:T(8,128)(2,1)S(1)}, u32[]{:S(2)}, u32[]{:S(2)}) collective-permute-start(bf16[8,128,256]{2,1,0:T(8,128)(2,1)S(1)} %collective-permute-done.3), channel_id=1, source_target_pairs={{0,448},{64,0},{384,320},{448,384},{1,449},{65,1},{385,321},{449,3... | collective-permute-start | bytes 1572872 | tf_op jit(solution)/shard_map/ppermute | solution.py:83
  113.1 12.4 %copy-start.2 = (bf16[128,64]{1,0:T(8,128)(2,1)S(1)}, bf16[128,64]{1,0:T(8,128)(2,1)}, u32[]{:S(2)}) copy-start(bf16[128,64]{1,0:T(8,128)(2,1)} %copy-done.1) | copy-start | bytes 49156
  113.1 12.4 %copy-start.4 = (bf16[128,64]{1,0:T(8,128)(2,1)S(1)}, bf16[128,64]{1,0:T(8,128)(2,1)}, u32[]{:S(2)}) copy-start(bf16[128,64]{1,0:T(8,128)(2,1)} %copy-done.3) | copy-start | bytes 49156
  120.7 15.9 %all-to-all-start.3 = ((bf16[4,16,2560]{2,1,0:T(8,128)(2,1)}), bf16[4,16,2560]{2,1,0:T(8,128)(2,1)S(1)}, u32[]{:S(2)}, u32[]{:S(2)}) async-start(bf16[4,16,2560]{2,1,0:T(8,128)(2,1)} %reduce_sum.84), calls=%async_computation.3 | async-start | bytes 655360 | tf_op jit(solution)/shard_map/all_to_all | solution.py:185
